TPU v7x, 128 devices: a whole 4x4x4 slice. The times are simulated.
128 devices in a mesh: dp: 8 (over z, core), ts: 16 (over y, x).
Axes of the slice: x: 4, y: 4, z: 4, core: 2. Of those that a mesh axis runs over, the one named last changes fastest.
Arguments:
- text_embed: bfloat16 [8, 1024, 4096], P('dp', None, 'ts'), may hold values from -6 to 6
- bridge: bfloat16 [128, 32, 4096], P('dp', None, 'ts'), may hold values from -6 to 6
- crystal_slot: int32 [128], P('dp'), may hold values from 0 to 8159, as said below
- segments: int32 [8, 1024], P('dp'), may hold values from 0 to 15, as said below
- attn_gain: float32 [4096], replicated, may hold values from 0.1 to 1.9
- w_query: bfloat16 [4096, 4096], P(None, 'ts'), as said below
- w_key: bfloat16 [4096, 1024], P(None, 'ts'), may hold values from -0.09375 to 0.09375
- w_value: bfloat16 [4096, 1024], P(None, 'ts'), may hold values from -0.09375 to 0.09375
- w_out: bfloat16 [4096, 4096], P('ts'), may hold values from -0.09375 to 0.09375
- mlp_gain: float32 [4096], replicated, may hold values from 0.1 to 1.9
- w_gate: bfloat16 [4096, 12288], P(None, 'ts'), may hold values from -0.09375 to 0.09375
- w_up: bfloat16 [4096, 12288], P(None, 'ts'), may hold values from -0.09375 to 0.09375
- w_down: bfloat16 [12288, 4096], P('ts'), may hold values from -0.0546875 to 0.0546875
Outputs:
- layer_out: bfloat16 [8, 1024, 4096], P('dp', 'ts')
Inputs may be any that keep to these rules, and one draw needn't show every extreme that they name: `segments`: each row starts at 0, never falls and names every document number of 0 to 15; every document holds at least 33 positions. `crystal_slot`: each crystal's 32 rows take the first 32 positions of one document, given as sequence * 1024 + that document's first position; every document takes exactly one crystal, and each sequence takes exactly 2 of the 16 crystals held by each index of dp. `w_query`: entries lie within plus or minus 104 / sqrt(4096).
All inputs are finite; a program needn't handle non-finite values.
Results may differ from a plain program's by a relative error of at most 0.025.
The roundings to bfloat16 on the way count: a program that leaves them out, or rounds other values in their place, can miss the bound.
Values may be sent and summed in bfloat16 or wider, within the bound.
No kernel may reach another device: no remote copies, remote signals or barrier semaphores. Data moves between devices by JAX's collectives and lax.ppermute only.
A program may use at most 128 MiB of HBM per device.

v0:
```python
import jax
import jax.numpy as jnp
from jax import lax
from jax.sharding import PartitionSpec as P

HD = 128
DOC_LEN = 64
norm_epsilon = 1e-05
rope_base = 500000.0
masked_score = -1e30


def partner_2(block, axis, apart):
    count = lax.axis_size(axis)
    route = []
    for low in range(count):
        high = low | 1 << apart
        if high != low and high < count:
            route += [(low, high), (high, low)]
    return lax.ppermute(block, axis, route)


def norm_rows(rows, gain):
    widened = rows.astype(jnp.float32)
    inverse_rms = lax.rsqrt(jnp.mean(widened * widened, axis=-1, keepdims=True) + norm_epsilon)
    return (widened * inverse_rms * gain).astype(jnp.bfloat16)


def rotate_pairs(values, positions, first_pair):
    pair_count = values.shape[-1] // 2
    exponent = 2.0 * (first_pair + jnp.arange(pair_count, dtype=jnp.int32)).astype(jnp.float32) / HD
    frequency = rope_base ** (-exponent)
    angles = positions.astype(jnp.float32)[:, None] * frequency[None, :]
    cosine = jnp.cos(angles)[:, None, :]
    sine_part = jnp.sin(angles)[:, None, :]
    paired = values.reshape(values.shape[0], values.shape[1], pair_count, 2)
    even_part = paired[..., 0]
    odd_part = paired[..., 1]
    new_even = even_part * cosine - odd_part * sine_part
    new_odd = even_part * sine_part + odd_part * cosine
    return jnp.stack([new_even, new_odd], axis=-1).reshape(values.shape)


def attend_block(query_block, query_segments, query_index, keys_full, values_full, segment_ids):
    scores = jnp.einsum(
        "qhd,kd->hqk", query_block, keys_full, preferred_element_type=jnp.float32
    ) * HD ** (-0.5)
    key_index = jnp.arange(keys_full.shape[0], dtype=jnp.int32)
    allowed = (query_segments[:, None] == segment_ids[None, :]) & (
        key_index[None, :] <= query_index[:, None]
    )
    scores = jnp.where(allowed[None], scores, masked_score)
    row_top = jnp.max(scores, axis=-1, keepdims=True)
    weights = jnp.exp(scores - row_top)
    probabilities = (weights / jnp.sum(weights, axis=-1, keepdims=True)).astype(jnp.bfloat16)
    mixed_rows = jnp.einsum(
        "hqk,kd->qhd", probabilities, values_full, preferred_element_type=jnp.float32
    )
    return mixed_rows.astype(jnp.bfloat16).reshape(query_block.shape[0], -1)


def shards(
    text_embed,
    bridge,
    crystal_slot,
    segments,
    attn_gain,
    w_query,
    w_key,
    w_value,
    w_out,
    mlp_gain,
    w_gate,
    w_up,
    w_down,
):
    seq_len = text_embed.shape[1]
    part_width = text_embed.shape[2]
    doc_count = seq_len // DOC_LEN
    bridge_len = bridge.shape[1]
    tok_rows = seq_len // lax.axis_size("ts")
    group_index = lax.axis_index("dp")
    ts_index = lax.axis_index("ts")
    segment_ids = segments[0]
    doc_numbers = jnp.arange(doc_count, dtype=jnp.int32)
    starts = jnp.sum((segment_ids[None, :] < doc_numbers[:, None]).astype(jnp.int32), axis=1)
    doc_match = segment_ids[:, None] == doc_numbers[None, :]
    positions = jnp.arange(seq_len, dtype=jnp.int32) - jnp.sum(
        jnp.where(doc_match, starts[None, :], 0), axis=1
    )
    flat_bridge = bridge.reshape(bridge.shape[0], bridge_len * part_width)
    arrived, arrived_slots = (
        lax.all_gather(flat_bridge, "dp", axis=0, tiled=True),
        lax.all_gather(crystal_slot, "dp", axis=0, tiled=True),
    )
    wanted = group_index * seq_len + starts
    picking = wanted[:, None] == arrived_slots[None, :]
    by_doc = jnp.dot(
        picking.astype(jnp.bfloat16), arrived, preferred_element_type=jnp.float32
    ).astype(jnp.bfloat16)
    by_doc = by_doc.reshape(doc_count * bridge_len, part_width)
    in_bridge = positions < bridge_len
    row_pick = (segment_ids * bridge_len + positions)[:, None] == jnp.arange(
        doc_count * bridge_len, dtype=jnp.int32
    )[None, :]
    row_pick = row_pick & in_bridge[:, None]
    filled = jnp.dot(
        row_pick.astype(jnp.bfloat16), by_doc, preferred_element_type=jnp.float32
    ).astype(jnp.bfloat16)
    own_part = jnp.where(in_bridge[:, None], filled, text_embed[0])
    packed = lax.all_gather(own_part, "ts", axis=1, tiled=True)
    normed = norm_rows(packed, attn_gain)
    heads_here = w_query.shape[1] // HD
    queries = jnp.dot(normed, w_query, preferred_element_type=jnp.float32).reshape(
        seq_len, heads_here, HD
    )
    queries = rotate_pairs(queries, positions, 0).astype(jnp.bfloat16)
    kv_cols = w_key.shape[1]
    upper_half = ts_index % 2 == 1
    key_half = jnp.dot(normed, w_key, preferred_element_type=jnp.float32).reshape(
        seq_len, 1, kv_cols
    )
    key_half = rotate_pairs(key_half, positions, ts_index % 2 * (kv_cols // 2))
    key_half = key_half.astype(jnp.bfloat16).reshape(seq_len, kv_cols)
    value_half = jnp.dot(normed, w_value, preferred_element_type=jnp.float32).astype(jnp.bfloat16)
    own_pair = jnp.concatenate([key_half, value_half], axis=1)
    partner = partner_2(own_pair, "ts", 0)
    lower_half = jnp.where(upper_half, partner, own_pair)
    higher = jnp.where(upper_half, own_pair, partner)
    keys_full = jnp.concatenate([lower_half[:, :kv_cols], higher[:, :kv_cols]], axis=1)
    values_full = jnp.concatenate([lower_half[:, kv_cols:], higher[:, kv_cols:]], axis=1)
    block_rows = min(512, seq_len)
    outputs = []
    for block_index in range(seq_len // block_rows):
        first_row = block_index * block_rows
        query_index = jnp.arange(first_row, first_row + block_rows, dtype=jnp.int32)
        outputs.append(
            attend_block(
                queries[first_row : first_row + block_rows],
                segment_ids[first_row : first_row + block_rows],
                query_index,
                keys_full,
                values_full,
                segment_ids,
            )
        )
    attended = jnp.concatenate(outputs, axis=0)
    mine_offset = ts_index * tok_rows
    partial_rows = jnp.dot(attended, w_out, preferred_element_type=jnp.float32)
    attn_sum = lax.psum(partial_rows.astype(jnp.bfloat16), "ts").astype(jnp.float32)
    after_all = (packed.astype(jnp.float32) + attn_sum).astype(jnp.bfloat16)
    after_mine = lax.dynamic_slice_in_dim(after_all, mine_offset, tok_rows, 0)
    normed_mlp = norm_rows(after_all, mlp_gain)
    gate_proj = jnp.dot(normed_mlp, w_gate, preferred_element_type=jnp.float32)
    up_proj = jnp.dot(normed_mlp, w_up, preferred_element_type=jnp.float32)
    hidden = (jax.nn.silu(gate_proj) * up_proj).astype(jnp.bfloat16)
    mlp_mine = lax.psum_scatter(
        jnp.dot(hidden, w_down, preferred_element_type=jnp.float32).astype(jnp.bfloat16),
        "ts",
        scatter_dimension=0,
        tiled=True,
    ).astype(jnp.float32)
    layer_rows = (after_mine.astype(jnp.float32) + mlp_mine).astype(jnp.bfloat16)
    return layer_rows.reshape(1, tok_rows, layer_rows.shape[1])


def solution(mesh):
    return jax.shard_map(
        shards,
        mesh=mesh,
        in_specs=(
            P("dp", None, "ts"),
            P("dp", None, "ts"),
            P("dp"),
            P("dp", None),
            P(),
            P(None, "ts"),
            P(None, "ts"),
            P(None, "ts"),
            P("ts", None),
            P(),
            P(None, "ts"),
            P(None, "ts"),
            P("ts", None),
        ),
        out_specs=P("dp", "ts", None),
        check_vma=False,
    )
```

profile of v0, /device:TPU:0, one launch (start us, length us, event | category | flops | bytes accessed | tf_op | source)
XLA Modules:
  0.0 462.7 jit_solution(8637387790045024165)
XLA Ops:
  11.4 10.6 %all-reduce = s32[128]{0:T(128)S(1)} all-reduce(s32[128]{0:T(128)S(1)} %dynamic-update-slice), channel_id=1, replica_groups=mesh['dp'=8,'ts'=16] {'dp'}, use_global_device_ids=true, to_apply=%add | all-reduce | flops 128 | bytes 1024
  24.3 12.6 %all-gather.3.cloned.1.call-done = bf16[128,8192]{1,0:T(8,128)(2,1)} async-done(((bf16[16,8192]{1,0:T(8,128)(2,1)}), bf16[128,8192]{1,0:T(8,128)(2,1)}) %all-gather.3.cloned.1.call-update) | async-done | bytes 2097168 | tf_op jit(solution)/shard_map/all_gather | solution.py:93
  37.0 2.0 convolution_convert_fusion
  39.1 2.7 fusion.36
  42.0 2.3 multiply_cosine_fusion
  45.9 74.7 %all-gather.5.cloned.1.call-done = bf16[1024,4096]{1,0:T(8,128)(2,1)} async-done(((bf16[1024,256]{1,0:T(8,128)(2,1)}), bf16[1024,4096]{1,0:T(8,128)(2,1)}) %all-gather.5.cloned.1.call-update) | async-done | bytes 8388624 | tf_op jit(solution)/shard_map/all_gather | solution.py:111
  120.6 5.1 %fusion.5 = f32[1024]{0:T(1024)S(1)} fusion(bf16[1024,4096]{1,0:T(8,128)(2,1)} %all-gather.5.cloned.1.call-done), kind=kLoop, calls=%fused_computation.10 | loop fusion | flops 12581888 | bytes 8392704 | tf_op jit(solution)/shard_map/reduce_sum | solution.py:25
  125.7 10.4 %fusion.7 = bf16[1024,4096]{1,0:T(8,128)(2,1)} fusion(bf16[1024,4096]{1,0:T(8,128)(2,1)} %all-gather.5.cloned.1.call-done, f32[4096]{0:T(1024)S(1)} %copy-done.8, f32[1024]{0:T(1024)S(1)} %add_rsqrt_fusion.1), kind=kLoop, calls=%fused_computation.12 | loop fusion | flops 16777216 | bytes 16797696 | tf_op jit(solution)/shard_map/convert_element_type | solution.py:26
  136.1 6.2 %convolution_convert_fusion.3 = bf16[1024,64]{0,1:T(8,128)(2,1)S(1)} fusion(bf16[1024,4096]{1,0:T(8,128)(2,1)} %fusion.7, bf16[4096,64]{0,1:T(8,128)(2,1)S(1)} %copy-done.4), kind=kOutput, calls=%fused_computation.48 | convolution fusion | flops 536936448 | bytes 9043968 | tf_op jit(solution)/shard_map/dot_general | solution.py:125
  142.4 2.7 fusion.103
  145.0 3.6 fusion.104
  155.5 2.1 subtract_convert_fusion
  158.9 2.7 collective-permute-done
  161.7 4.8 %fusion.98 = (f32[2,512]{1,0:T(2,128)S(1)}, f32[2,512,1024]{1,2,0:T(8,128)}) fusion(pred[512,1024]{0,1:T(8,128)(4,1)} %get-tuple-element.25, bf16[512,2,128]{0,1,2:T(2,128)(2,1)} %bitcast.86, bf16[1024,64]{0,1:T(8,128)(2,1)S(1)} %get-tuple-element.35, bf16[1024,64]{0,1:T(8,128)(2,1)S(1)} %get-tuple-element.18), kind=kOutput, calls=%fused_computation.119 | convolution fusion | flops 273155072 | bytes 5246976 | tf_op jit(solution)/shard_map/sub | solution.py:54
  166.5 3.7 fusion.93
  170.2 2.8 fusion.40
  174.2 5.6 %convolution_convert_fusion.2 = bf16[1024,4096]{1,0:T(8,128)(2,1)} fusion(bf16[256,4096]{1,0:T(8,128)(2,1)S(1)} %copy-done, bf16[512,256]{0,1:T(8,128)(2,1)S(1)} %bitcast.83, bf16[512,256]{0,1:T(8,128)(2,1)S(1)} %bitcast.82), kind=kOutput, calls=%fused_computation.16 | convolution fusion | flops 2152726528 | bytes 11010048 | tf_op jit(solution)/shard_map/dot_general | solution.py:149
  179.8 140.8 %all-reduce.3.cloned.1.call-done = bf16[1024,4096]{1,0:T(8,128)(2,1)} async-done(((bf16[1024,4096]{1,0:T(8,128)(2,1)}), bf16[1024,4096]{1,0:T(8,128)(2,1)}) %all-reduce.3.cloned.1.call-update) | async-done | bytes 8388624 | tf_op jit(solution)/shard_map/psum | solution.py:150
  320.6 8.0 %fusion.2 = (f32[1024]{0:T(1024)S(1)}, bf16[1024,4096]{1,0:T(8,128)(2,1)S(1)}) fusion(bf16[1024,4096]{1,0:T(8,128)(2,1)} %all-reduce.3.cloned.1.call-done, bf16[1024,4096]{1,0:T(8,128)(2,1)} %all-gather.5.cloned.1.call-done), kind=kLoop, calls=%fused_computation.7 | loop fusion | flops 29359104 | bytes 25169920 | tf_op jit(solution)/shard_map/reduce_sum | solution.py:25
  328.7 3.2 copy-done.3
  331.9 11.3 %fusion.11 = f32[1024,768]{1,0:T(8,128)} fusion(bf16[4096,768]{1,0:T(8,128)(2,1)} %param.24, bf16[1024,4096]{1,0:T(8,128)(2,1)S(1)} %get-tuple-element.6, f32[4096]{0:T(1024)S(1)} %copy-done.10, f32[1024]{0:T(1024)S(1)} %add_rsqrt_fusion), kind=kOutput, calls=%fused_computation.26 | convolution fusion | flops 6459228160 | bytes 17846272 | tf_op jit(solution)/shard_map/dot_general | solution.py:155
  343.2 26.4 %convolution_convert_fusion.1 = bf16[1024,4096]{1,0:T(8,128)(2,1)} fusion(bf16[768,4096]{1,0:T(8,128)(2,1)} %param.25, f32[1024,768]{1,0:T(8,128)} %fusion.11, bf16[4096,768]{1,0:T(8,128)(2,1)} %param.23, bf16[1024,4096]{1,0:T(8,128)(2,1)} %copy-done.3, f32[4096]{0:T(1024)S(1)} %copy-done.10, f32[1024]{0:T(1024)S(1)} %add_rsqrt_fusion), kind=kOutput, calls=%fused_computation.15 | convolution fusion | flops 12910592000 | bytes 32526336 | tf_op jit(solution)/shard_map/dot_general | solution.py:158
  369.6 84.2 %reduce-scatter.2.cloned.1.call-done = bf16[64,4096]{1,0:T(8,128)(2,1)} async-done(((bf16[1024,4096]{1,0:T(8,128)(2,1)}), bf16[64,4096]{1,0:T(8,128)(2,1)}) %reduce-scatter.2.cloned.1.call-update) | async-done | bytes 524304 | tf_op jit(solution)/shard_map/reduce_scatter | solution.py:157
  453.8 2.1 fusion.43
  (62 shorter events, 17.8 us)
Async XLA Ops:
  6.5 167.6 %copy-start = (bf16[256,4096]{1,0:T(8,128)(2,1)S(1)}, bf16[256,4096]{1,0:T(8,128)(2,1)}, u32[]{:S(2)}) copy-start(bf16[256,4096]{1,0:T(8,128)(2,1)} %param.21) | copy-start | bytes 6291460
  6.5 35.4 %copy-start.7 = (s32[1,1024]{1,0:T(1,128)S(1)}, s32[1,1024]{1,0:T(1,128)}, u32[]{:S(2)}) copy-start(s32[1,1024]{1,0:T(1,128)} %param.16) | copy-start | bytes 12292
  6.5 30.4 %all-gather.3.cloned.1.call-start = ((), (), s32[]{:S(2)}) async-start(), calls=%async_computation.1 | async-start | bytes 2359296 | tf_op jit(solution)/shard_map/all_gather | solution.py:93
  8.5 112.1 %all-gather.5.cloned.1.call-start = ((), (), s32[]{:S(2)}) async-start(), calls=%async_computation.2 | async-start | bytes 8912896 | tf_op jit(solution)/shard_map/all_gather | solution.py:111
  39.1 86.6 %copy-start.8 = (f32[4096]{0:T(1024)S(1)}, f32[4096]{0:T(1024)}, u32[]{:S(2)}) copy-start(f32[4096]{0:T(1024)} %param.17) | copy-start | bytes 49156
  41.9 278.8 %all-reduce.3.cloned.1.call-start = ((), (), s32[]{:S(2)}) async-start(), calls=%async_computation.3 | async-start | bytes 16777216 | tf_op jit(solution)/shard_map/psum | solution.py:150
  125.7 10.4 %copy-start.4 = (bf16[4096,64]{0,1:T(8,128)(2,1)S(1)}, bf16[4096,64]{0,1:T(8,128)(2,1)}, u32[]{:S(2)}) copy-start(bf16[4096,64]{0,1:T(8,128)(2,1)} %param.20) | copy-start | bytes 1572868
  136.1 6.2 %copy-start.2 = (bf16[1024,4096]{1,0:T(8,128)(2,1)S(1)}, bf16[1024,4096]{1,0:T(8,128)(2,1)}, u32[]{:S(2)}) copy-start(bf16[1024,4096]{1,0:T(8,128)(2,1)} %fusion.7) | copy-start | bytes 25165828
  136.1 6.2 %copy-start.5 = (bf16[4096,64]{0,1:T(8,128)(2,1)S(1)}, bf16[4096,64]{0,1:T(8,128)(2,1)}, u32[]{:S(2)}) copy-start(bf16[4096,64]{0,1:T(8,128)(2,1)} %param.19) | copy-start | bytes 1572868
  142.3 2.7 copy-start.9
  154.3 7.3 %collective-permute-start = (bf16[1024,128]{0,1:T(8,128)(2,1)S(1)}, bf16[1024,128]{0,1:T(8,128)(2,1)S(1)}, u32[]{:S(2)}, u32[]{:S(2)}) collective-permute-start(bf16[1024,128]{0,1:T(8,128)(2,1)S(1)} %pad_maximum_fusion.1), channel_id=1, source_target_pairs={{0,1},{1,0},{2,3},{3,2},{4,5},{5,4},{6,7},{7,6},{8,9},{9,8},{10,11... | collective-permute-start | bytes 786440 | tf_op jit(solution)/shard_map/ppermute | solution.py:20
  157.6 8.9 %copy-start.6 = (pred[512,1024]{0,1:T(8,128)(4,1)S(1)}, pred[512,1024]{0,1:T(8,128)(4,1)}, u32[]{:S(2)}) copy-start(pred[512,1024]{0,1:T(8,128)(4,1)} %get-tuple-element.26) | copy-start | bytes 1572868
  170.2 3.4 copy-start.11
  179.8 152.1 %copy-start.10 = (f32[4096]{0:T(1024)S(1)}, f32[4096]{0:T(1024)}, u32[]{:S(2)}) copy-start(f32[4096]{0:T(1024)} %param.22) | copy-start | bytes 49156
  179.8 274.0 %reduce-scatter.2.cloned.1.call-start = ((), (), s32[]{:S(2)}) async-start(), calls=%async_computation.4 | async-start | bytes 8912896 | tf_op jit(solution)/shard_map/reduce_scatter | solution.py:157
  328.7 3.2 copy-start.3
  343.2 112.7 %copy-start.1 = (bf16[256,4096]{1,0:T(8,128)(2,1)S(1)}, bf16[256,4096]{1,0:T(8,128)(2,1)}, u32[]{:S(2)}) copy-start(bf16[256,4096]{1,0:T(8,128)(2,1)} %param.21) | copy-start | bytes 6291460
Sparse Core Ops, SparseCore 0:
  9.1 27.8 all-gather.2
  42.0 78.5 all-gather.4
  179.9 140.6 all-reduce.2
  369.7 84.0 reduce-scatter.1
where the time goes:
time: 466 us; the launch traced here: 463 us
  waiting for transfers between devices  315 us (68%)
  matrix products  72.3 us (16%)
  other arithmetic  35.9 us (8%)
  between operations  14.3 us (3%)
  local copies, waits for them, and re-layouts  13.2 us (3%)
  blocking collectives  10.6 us (2%)
    psum x1, waiting for transfers between devices, shards(): lax.psum(partial_rows.astype(jnp.bfloat16), 'ts').astype(jnp.float32)  141 us
    reduce_scatter x1, waiting for transfers between devices, shards(): lax.psum_scatter(jnp.dot(hidden, w_down, preferred_element_type=jnp.float...  84.2 us
    all_gather x1, waiting for transfers between devices, shards(): packed = lax.all_gather(own_part, 'ts', axis=1, tiled=True)  74.7 us
    dot_general x1, matrix products, shards(): jnp.dot(hidden, w_down, preferred_element_type=jnp.float32)  26.4 us
    reduce_sum x2, other arithmetic, norm_rows(): jnp.mean(widened * widened, axis=-1, keepdims=True) + norm_epsilon  13.1 us
    all_gather x1, waiting for transfers between devices, shards(): lax.all_gather(flat_bridge, 'dp', axis=0, tiled=True)  12.6 us
    dot_general x1, matrix products, shards(): up_proj = jnp.dot(normed_mlp, w_up, preferred_element_type=jnp.float32)  11.3 us
    unnamed x1, blocking collectives  10.6 us
  transfers between devices with their start and end apart: 5, of which 5 were waited for; matrix products, arithmetic and copies ran while one was open for 3% of the time, Pallas kernels for 0%

commit v1 on v0

--- a/solution.py
+++ b/solution.py
@@ -8,6 +8,28 @@
 norm_epsilon = 1e-05
 rope_base = 500000.0
 masked_score = -1e30
+
+
+def joined_along(parts, dim):
+    parts = jnp.moveaxis(parts, 0, dim)
+    shape = parts.shape
+    return parts.reshape(*shape[:dim], shape[dim] * shape[dim + 1], *shape[dim + 2 :])
+
+
+def gather_around(shard, axis, dim):
+    length = lax.axis_size(axis)
+    pairs = [(i, (i + 1) % length) for i in range(length)]
+    back = [(b, a) for a, b in pairs]
+    lower, upper = ([], [])
+    for step in range(length - 1):
+        if step % 2 == 0:
+            lower.append(lax.ppermute(lower[-1] if lower else shard, axis, pairs))
+        else:
+            upper.append(lax.ppermute(upper[-1] if upper else shard, axis, back))
+    blocks = jnp.stack([*lower[::-1], shard, *upper])
+    shift = lax.axis_index(axis) - len(lower)
+    blocks = blocks[(jnp.arange(length) - shift) % length]
+    return joined_along(blocks, dim)
 
 
 def partner_2(block, axis, apart):
@@ -90,7 +112,7 @@
     )
     flat_bridge = bridge.reshape(bridge.shape[0], bridge_len * part_width)
     arrived, arrived_slots = (
-        lax.all_gather(flat_bridge, "dp", axis=0, tiled=True),
+        gather_around(flat_bridge, "dp", 0),
         lax.all_gather(crystal_slot, "dp", axis=0, tiled=True),
     )
     wanted = group_index * seq_len + starts

time: 466 us -> 484 us (1.039)
  local copies, waits for them, and re-layouts: 13.2 us -> 25.5 us
  starting transfers between devices: 1.38 us -> 7.91 us
    ppermute x0 -> x7, waiting for transfers between devices: none -> 13.6 us  [the longest x4 13.5 us: gather_around(): lower.append(lax.ppermute(lower[-1] if lower else shard, axis, pairs))]
    all_gather x1 -> x0, waiting for transfers between devices: 12.6 us -> none  [shards(): lax.all_gather(flat_bridge, 'dp', axis=0, tiled=True)]
    ppermute x0 -> x7, starting transfers between devices: none -> 6.57 us  [the longest x3 6.54 us: gather_around(): upper.append(lax.ppermute(upper[-1] if upper else shard, axis, back))]
    unnamed x28 -> x41, local copies, waits for them, and re-layouts: 8.03 us -> 14.2 us
  transfers between devices with their start and end apart: 5 -> 11, of which waited for: 5 -> 7; matrix products, arithmetic and copies ran while one was open for 3% -> 4% of each run, Pallas kernels for 0% -> 0%
where the time goes in v1:
time: 484 us; the launch traced here: 481 us
  waiting for transfers between devices  314 us (65%)
  matrix products  73.2 us (15%)
  other arithmetic  36 us (7%)
  local copies, waits for them, and re-layouts  25.5 us (5%)
  between operations  14.3 us (3%)
  blocking collectives  9.31 us (2%)
  starting transfers between devices  7.91 us (2%)
    psum x1, waiting for transfers between devices, shards(): lax.psum(partial_rows.astype(jnp.bfloat16), 'ts').astype(jnp.float32)  141 us
    reduce_scatter x1, waiting for transfers between devices, shards(): lax.psum_scatter(jnp.dot(hidden, w_down, preferred_element_type=jnp.float...  84 us
    all_gather x1, waiting for transfers between devices, shards(): packed = lax.all_gather(own_part, 'ts', axis=1, tiled=True)  73.4 us
    dot_general x1, matrix products, shards(): jnp.dot(hidden, w_down, preferred_element_type=jnp.float32)  26.3 us
    unnamed x41, local copies, waits for them, and re-layouts  14.2 us
    ppermute x4, waiting for transfers between devices, gather_around(): lower.append(lax.ppermute(lower[-1] if lower else shard, axis, pairs))  13.5 us
    reduce_sum x2, other arithmetic, norm_rows(): jnp.mean(widened * widened, axis=-1, keepdims=True) + norm_epsilon  13.1 us
    dot_general x1, matrix products, shards(): up_proj = jnp.dot(normed_mlp, w_up, preferred_element_type=jnp.float32)  11.3 us
  transfers between devices with their start and end apart: 11, of which 7 were waited for; matrix products, arithmetic and copies ran while one was open for 4% of the time, Pallas kernels for 0%

profile of v1, /device:TPU:0, one launch (start us, length us, event | category | flops | bytes accessed | tf_op | source)
XLA Modules:
  0.0 480.6 jit_solution(363233375653968150)
XLA Ops:
  7.8 3.6 collective-permute-start.4
  12.2 3.2 collective-permute-done
  16.2 6.2 %collective-permute-done.1 = bf16[16,8192]{1,0:T(8,128)(2,1)S(1)} collective-permute-done((bf16[16,8192]{1,0:T(8,128)(2,1)S(1)}, bf16[16,8192]{1,0:T(8,128)(2,1)S(1)}, u32[]{:S(2)}, u32[]{:S(2)}) %collective-permute-start.1) | collective-permute-done | bytes 262176 | tf_op jit(solution)/shard_map/ppermute | solution.py:26
  22.5 3.0 collective-permute-start.5
  25.4 4.1 collective-permute-done.2
  33.4 9.3 %all-reduce = s32[128]{0:T(128)S(1)} all-reduce(s32[128]{0:T(128)S(1)} %dynamic-update-slice), channel_id=1, replica_groups=mesh['dp'=8,'ts'=16] {'dp'}, use_global_device_ids=true, to_apply=%add | all-reduce | flops 128 | bytes 1024
  51.1 3.6 gather_fusion
  56.9 2.7 fusion.36
  63.7 73.4 %all-gather.2.cloned.1.call-done = bf16[1024,4096]{1,0:T(8,128)(2,1)} async-done(((bf16[1024,256]{1,0:T(8,128)(2,1)}), bf16[1024,4096]{1,0:T(8,128)(2,1)}) %all-gather.2.cloned.1.call-update) | async-done | bytes 8388624 | tf_op jit(solution)/shard_map/all_gather | solution.py:133
  137.1 5.1 %fusion.5 = f32[1024]{0:T(1024)S(1)} fusion(bf16[1024,4096]{1,0:T(8,128)(2,1)} %all-gather.2.cloned.1.call-done), kind=kLoop, calls=%fused_computation.11 | loop fusion | flops 12581888 | bytes 8392704 | tf_op jit(solution)/shard_map/reduce_sum | solution.py:47
  142.2 10.4 %fusion.7 = bf16[1024,4096]{1,0:T(8,128)(2,1)} fusion(bf16[1024,4096]{1,0:T(8,128)(2,1)} %all-gather.2.cloned.1.call-done, f32[4096]{0:T(1024)S(1)} %copy-done.11, f32[1024]{0:T(1024)S(1)} %add_rsqrt_fusion.1), kind=kLoop, calls=%fused_computation.13 | loop fusion | flops 16777216 | bytes 16797696 | tf_op jit(solution)/shard_map/convert_element_type | solution.py:48
  152.6 6.2 %convolution_convert_fusion.3 = bf16[1024,64]{0,1:T(8,128)(2,1)S(1)} fusion(bf16[1024,4096]{1,0:T(8,128)(2,1)} %fusion.7, bf16[4096,64]{0,1:T(8,128)(2,1)S(1)} %copy-done.4), kind=kOutput, calls=%fused_computation.49 | convolution fusion | flops 536936448 | bytes 9043968 | tf_op jit(solution)/shard_map/dot_general | solution.py:147
  158.8 2.7 fusion.105
  161.5 3.6 fusion.106
  178.9 4.9 %fusion.100 = (f32[2,512]{1,0:T(2,128)S(1)}, f32[2,512,1024]{1,2,0:T(8,128)}) fusion(pred[512,1024]{0,1:T(8,128)(4,1)S(1)} %copy-done.7, bf16[512,2,128]{0,1,2:T(2,128)(2,1)} %bitcast.105, bf16[1024,64]{0,1:T(8,128)(2,1)} %get-tuple-element.35, bf16[1024,64]{0,1:T(8,128)(2,1)} %get-tuple-element.18), kind=kOutput, calls=%fused_computation.135 | convolution fusion | flops 273155072 | bytes 5246976 | tf_op jit(solution)/shard_map/sub | solution.py:76
  183.8 4.7 fusion.95
  188.4 2.8 fusion.40
  192.4 5.6 %convolution_convert_fusion.2 = bf16[1024,4096]{1,0:T(8,128)(2,1)} fusion(bf16[256,4096]{1,0:T(8,128)(2,1)S(1)} %copy-done, bf16[512,256]{0,1:T(8,128)(2,1)S(1)} %bitcast.101, bf16[512,256]{0,1:T(8,128)(2,1)S(1)} %bitcast.100), kind=kOutput, calls=%fused_computation.17 | convolution fusion | flops 2152726528 | bytes 11010048 | tf_op jit(solution)/shard_map/dot_general | solution.py:171
  198.1 140.8 %all-reduce.3.cloned.1.call-done = bf16[1024,4096]{1,0:T(8,128)(2,1)} async-done(((bf16[1024,4096]{1,0:T(8,128)(2,1)}), bf16[1024,4096]{1,0:T(8,128)(2,1)}) %all-reduce.3.cloned.1.call-update) | async-done | bytes 8388624 | tf_op jit(solution)/shard_map/psum | solution.py:172
  338.9 8.0 %fusion.2 = (f32[1024]{0:T(1024)S(1)}, bf16[1024,4096]{1,0:T(8,128)(2,1)S(1)}) fusion(bf16[1024,4096]{1,0:T(8,128)(2,1)} %all-reduce.3.cloned.1.call-done, bf16[1024,4096]{1,0:T(8,128)(2,1)} %all-gather.2.cloned.1.call-done), kind=kLoop, calls=%fused_computation.8 | loop fusion | flops 29359104 | bytes 25169920 | tf_op jit(solution)/shard_map/reduce_sum | solution.py:47
  346.9 3.2 copy-done.3
  350.1 11.3 %fusion.11 = f32[1024,768]{1,0:T(8,128)} fusion(bf16[4096,768]{1,0:T(8,128)(2,1)} %param.24, bf16[1024,4096]{1,0:T(8,128)(2,1)S(1)} %get-tuple-element.6, f32[4096]{0:T(1024)S(1)} %copy-done.13, f32[1024]{0:T(1024)S(1)} %add_rsqrt_fusion), kind=kOutput, calls=%fused_computation.27 | convolution fusion | flops 6459228160 | bytes 17846272 | tf_op jit(solution)/shard_map/dot_general | solution.py:177
  361.4 26.3 %convolution_convert_fusion.1 = bf16[1024,4096]{1,0:T(8,128)(2,1)} fusion(bf16[768,4096]{1,0:T(8,128)(2,1)} %param.25, f32[1024,768]{1,0:T(8,128)} %fusion.11, bf16[4096,768]{1,0:T(8,128)(2,1)} %param.23, bf16[1024,4096]{1,0:T(8,128)(2,1)} %copy-done.3, f32[4096]{0:T(1024)S(1)} %copy-done.13, f32[1024]{0:T(1024)S(1)} %add_rsqrt_fusion), kind=kOutput, calls=%fused_computation.16 | convolution fusion | flops 12910592000 | bytes 32526336 | tf_op jit(solution)/shard_map/dot_general | solution.py:180
  387.7 84.0 %reduce-scatter.2.cloned.1.call-done = bf16[64,4096]{1,0:T(8,128)(2,1)} async-done(((bf16[1024,4096]{1,0:T(8,128)(2,1)}), bf16[64,4096]{1,0:T(8,128)(2,1)}) %reduce-scatter.2.cloned.1.call-update) | async-done | bytes 524304 | tf_op jit(solution)/shard_map/reduce_scatter | solution.py:179
  (91 shorter events, 37.7 us)
Async XLA Ops:
  6.5 185.8 %copy-start = (bf16[256,4096]{1,0:T(8,128)(2,1)S(1)}, bf16[256,4096]{1,0:T(8,128)(2,1)}, u32[]{:S(2)}) copy-start(bf16[256,4096]{1,0:T(8,128)(2,1)} %param.21) | copy-start | bytes 6291460
  6.5 130.5 %all-gather.2.cloned.1.call-start = ((), (), s32[]{:S(2)}) async-start(), calls=%async_computation.1 | async-start | bytes 8912896 | tf_op jit(solution)/shard_map/all_gather | solution.py:133
  7.8 7.6 %collective-permute-start = (bf16[16,8192]{1,0:T(8,128)(2,1)S(1)}, bf16[16,8192]{1,0:T(8,128)(2,1)S(1)}, u32[]{:S(2)}, u32[]{:S(2)}) collective-permute-start(bf16[16,8192]{1,0:T(8,128)(2,1)S(1)} %bitcast.102), channel_id=1, source_target_pairs={{0,16},{16,32},{32,48},{48,64},{64,80},{80,96},{96,112},{112,0},{1... | collective-permute-start | bytes 786440 | tf_op jit(solution)/shard_map/ppermute | solution.py:26
  7.8 14.6 %collective-permute-start.4 = (bf16[16,8192]{1,0:T(8,128)(2,1)S(1)}, bf16[16,8192]{1,0:T(8,128)(2,1)S(1)}, u32[]{:S(2)}, u32[]{:S(2)}) collective-permute-start(bf16[16,8192]{1,0:T(8,128)(2,1)S(1)} %bitcast.103), channel_id=1, source_target_pairs={{16,0},{32,16},{48,32},{64,48},{80,64},{96,80},{112,96},{0,112},{1... | collective-permute-start | bytes 786440 | tf_op jit(solution)/shard_map/ppermute | solution.py:28
  15.4 7.0 %collective-permute-start.1 = (bf16[16,8192]{1,0:T(8,128)(2,1)S(1)}, bf16[16,8192]{1,0:T(8,128)(2,1)S(1)}, u32[]{:S(2)}, u32[]{:S(2)}) collective-permute-start(bf16[16,8192]{1,0:T(8,128)(2,1)S(1)} %collective-permute-done), channel_id=1, source_target_pairs={{0,16},{16,32},{32,48},{48,64},{64,80},{80,96},{96,112},{112,0},{1... | collective-permute-start | bytes 786440 | tf_op jit(solution)/shard_map/ppermute | solution.py:26
  22.4 7.1 %collective-permute-start.2 = (bf16[16,8192]{1,0:T(8,128)(2,1)S(1)}, bf16[16,8192]{1,0:T(8,128)(2,1)}, u32[]{:S(2)}, u32[]{:S(2)}) collective-permute-start(bf16[16,8192]{1,0:T(8,128)(2,1)S(1)} %collective-permute-done.1), channel_id=1, source_target_pairs={{0,16},{16,32},{32,48},{48,64},{64,80},{80,96},{96,112},{112,0},{1... | collective-permute-start | bytes 786440 | tf_op jit(solution)/shard_map/ppermute | solution.py:26
  22.5 20.9 %collective-permute-start.5 = (bf16[16,8192]{1,0:T(8,128)(2,1)S(1)}, bf16[16,8192]{1,0:T(8,128)(2,1)S(1)}, u32[]{:S(2)}, u32[]{:S(2)}) collective-permute-start(bf16[16,8192]{1,0:T(8,128)(2,1)S(1)} %collective-permute-done.4), channel_id=1, source_target_pairs={{16,0},{32,16},{48,32},{64,48},{80,64},{96,80},{112,96},{0,112},{1... | collective-permute-start | bytes 786440 | tf_op jit(solution)/shard_map/ppermute | solution.py:28
  29.5 13.9 %collective-permute-start.3 = (bf16[16,8192]{1,0:T(8,128)(2,1)}, bf16[16,8192]{1,0:T(8,128)(2,1)}, u32[]{:S(2)}, u32[]{:S(2)}) collective-permute-start(bf16[16,8192]{1,0:T(8,128)(2,1)} %collective-permute-done.2), channel_id=1, source_target_pairs={{0,16},{16,32},{32,48},{48,64},{64,80},{80,96},{96,112},{112,0},{1... | collective-permute-start | bytes 786440 | tf_op jit(solution)/shard_map/ppermute | solution.py:26
  43.4 7.0 %collective-permute-start.6 = (bf16[16,8192]{1,0:T(8,128)(2,1)S(1)}, bf16[16,8192]{1,0:T(8,128)(2,1)S(1)}, u32[]{:S(2)}, u32[]{:S(2)}) collective-permute-start(bf16[16,8192]{1,0:T(8,128)(2,1)S(1)} %collective-permute-done.5), channel_id=1, source_target_pairs={{16,0},{32,16},{48,32},{64,48},{80,64},{96,80},{112,96},{0,112},{1... | collective-permute-start | bytes 786440 | tf_op jit(solution)/shard_map/ppermute | solution.py:28
  51.1 8.6 %copy-start.10 = (s32[1,1024]{1,0:T(1,128)S(1)}, s32[1,1024]{1,0:T(1,128)}, u32[]{:S(2)}) copy-start(s32[1,1024]{1,0:T(1,128)} %param.16) | copy-start | bytes 12292
  59.6 279.2 %all-reduce.3.cloned.1.call-start = ((), (), s32[]{:S(2)}) async-start(), calls=%async_computation.2 | async-start | bytes 16777216 | tf_op jit(solution)/shard_map/psum | solution.py:172
  63.7 78.5 %copy-start.11 = (f32[4096]{0:T(1024)S(1)}, f32[4096]{0:T(1024)}, u32[]{:S(2)}) copy-start(f32[4096]{0:T(1024)} %param.17) | copy-start | bytes 49156
  142.2 10.4 %copy-start.4 = (bf16[4096,64]{0,1:T(8,128)(2,1)S(1)}, bf16[4096,64]{0,1:T(8,128)(2,1)}, u32[]{:S(2)}) copy-start(bf16[4096,64]{0,1:T(8,128)(2,1)} %param.20) | copy-start | bytes 1572868
  152.6 6.2 %copy-start.2 = (bf16[1024,4096]{1,0:T(8,128)(2,1)S(1)}, bf16[1024,4096]{1,0:T(8,128)(2,1)}, u32[]{:S(2)}) copy-start(bf16[1024,4096]{1,0:T(8,128)(2,1)} %fusion.7) | copy-start | bytes 25165828
  152.6 6.2 %copy-start.5 = (bf16[4096,64]{0,1:T(8,128)(2,1)S(1)}, bf16[4096,64]{0,1:T(8,128)(2,1)}, u32[]{:S(2)}) copy-start(bf16[4096,64]{0,1:T(8,128)(2,1)} %param.19) | copy-start | bytes 1572868
  170.7 8.2 %copy-start.7 = (pred[512,1024]{0,1:T(8,128)(4,1)S(1)}, pred[512,1024]{0,1:T(8,128)(4,1)}, u32[]{:S(2)}) copy-start(pred[512,1024]{0,1:T(8,128)(4,1)} %get-tuple-element.25) | copy-start | bytes 1572868
  170.8 7.3 %collective-permute-start.7 = (bf16[1024,128]{0,1:T(8,128)(2,1)S(1)}, bf16[1024,128]{0,1:T(8,128)(2,1)S(1)}, u32[]{:S(2)}, u32[]{:S(2)}) collective-permute-start(bf16[1024,128]{0,1:T(8,128)(2,1)S(1)} %pad_maximum_fusion.1), channel_id=1, source_target_pairs={{0,1},{1,0},{2,3},{3,2},{4,5},{5,4},{6,7},{7,6},{8,9},{9,8},{10,11... | collective-permute-start | bytes 786440 | tf_op jit(solution)/shard_map/ppermute | solution.py:42
  178.9 4.9 %copy-start.6 = (pred[512,1024]{0,1:T(8,128)(4,1)S(1)}, pred[512,1024]{0,1:T(8,128)(4,1)}, u32[]{:S(2)}) copy-start(pred[512,1024]{0,1:T(8,128)(4,1)} %get-tuple-element.26) | copy-start | bytes 1572868
  178.9 4.9 %copy-start.8 = (bf16[512,2,64,2]{0,1,3,2:T(2,128)(2,1)S(1)}, bf16[512,2,64,2]{0,1,3,2:T(2,128)(2,1)}, u32[]{:S(2)}) copy-start(bf16[512,2,64,2]{0,1,3,2:T(2,128)(2,1)} %get-tuple-element.12) | copy-start | bytes 786436
  183.8 4.7 copy-start.9
  188.4 3.4 copy-start.14
  198.0 152.1 %copy-start.13 = (f32[4096]{0:T(1024)S(1)}, f32[4096]{0:T(1024)}, u32[]{:S(2)}) copy-start(f32[4096]{0:T(1024)} %param.22) | copy-start | bytes 49156
  198.0 273.7 %reduce-scatter.2.cloned.1.call-start = ((), (), s32[]{:S(2)}) async-start(), calls=%async_computation.3 | async-start | bytes 8912896 | tf_op jit(solution)/shard_map/reduce_scatter | solution.py:179
  387.6 86.2 %copy-start.1 = (bf16[256,4096]{1,0:T(8,128)(2,1)S(1)}, bf16[256,4096]{1,0:T(8,128)(2,1)}, u32[]{:S(2)}) copy-start(bf16[256,4096]{1,0:T(8,128)(2,1)} %param.21) | copy-start | bytes 6291460
  (2 other events, 5.9 us)
Sparse Core Ops, SparseCore 0:
  59.8 77.2 all-gather.1
  198.1 140.6 all-reduce.2
  387.8 83.8 reduce-scatter.1
